TPU v7x, 32 devices: a whole 2x2x4 slice. The times are simulated.
32 devices in a mesh: row: 4 (over x, core), col: 8 (over z, y).
Axes of the slice: x: 2, y: 2, z: 4, core: 2. Of those that a mesh axis runs over, the one named last changes fastest.
Arguments:
- embed: bfloat16 [1024, 768], P(('row', 'col'))
- beta: bfloat16 [1024], P(('row', 'col')), may hold values from 16 to 400
- block_mask: int32 [8, 8], P('row'), may hold values from 0 to 1, as said below
- counts: int32 [8], replicated, may hold values from 2 to 128
- probes: float32 [64, 1024], P(None, ('row', 'col')), may hold values from -6 to 6
Outputs:
- spectral: float32 [64, 1024], P(None, ('row', 'col'))
Inputs may be any that keep to these rules, and one draw needn't show every extreme that they name: `block_mask`: every diagonal entry is 1.
All inputs are finite; a program needn't handle non-finite values.
Results may differ from a plain program's by a relative error of at most 0.012.
The roundings to bfloat16 on the way count: a program that leaves them out, or rounds other values in their place, can miss the bound.
Values may be sent and summed in bfloat16 or wider, within the bound.
No kernel may reach another device: no remote copies, remote signals or barrier semaphores. Data moves between devices by JAX's collectives and lax.ppermute only.
A program may use at most 64 MiB of HBM per device.

v0:
```python
import jax
import jax.numpy as jnp
from jax import lax
from jax.sharding import PartitionSpec as P

ITERS = 2


def spread(shard, axis, root):
    mine = lax.axis_index(axis) == root
    return lax.psum(jnp.where(mine, shard, jnp.zeros_like(shard)), axis)


def own_piece(totals, col_ratio, n_row, row_index, col_index):
    shard_len = totals.shape[1] // n_row
    chosen = jnp.zeros_like(totals)
    for root_k in range(col_ratio):
        received = spread(totals, "col", col_ratio * row_index + root_k)
        chosen = jnp.where(col_index // n_row == root_k, received, chosen)
    return lax.dynamic_slice_in_dim(chosen, col_index % n_row * shard_len, shard_len, 1)


def body(embed, beta, block_mask, counts, probes):
    n_row = lax.axis_size("row")
    n_col = lax.axis_size("col")
    col_ratio = n_col // n_row
    row_index = lax.axis_index("row")
    col_index = lax.axis_index("col")
    shard_len, feat_width = embed.shape
    row_files = shard_len * n_col
    col_files = shard_len * n_row
    values = embed.astype(jnp.float32)
    unit_vec = (
        values * lax.rsqrt(jnp.mean(values * values, axis=1, keepdims=True) + 1e-06)
    ).astype(jnp.bfloat16)
    unit_rows, beta_rows = (
        lax.all_gather(unit_vec, "col", axis=0, tiled=True),
        lax.all_gather(beta, "col", axis=0, tiled=True),
    )
    half_pick = col_index % col_ratio
    col_seq = lax.iota(jnp.int32, col_files)
    unit_cols = spread(
        lax.dynamic_slice_in_dim(unit_rows, half_pick * col_files, col_files, 0),
        "row",
        col_index // col_ratio,
    )
    col_ids = col_index * col_files + col_seq
    gram_tile = lax.dot_general(
        unit_rows, unit_cols, (((1,), (1,)), ((), ())), preferred_element_type=jnp.float32
    )
    scores = gram_tile * (beta_rows.astype(jnp.float32) / feat_width)[:, None]
    row_blocks = block_mask.shape[0]
    blk_size = row_files // row_blocks
    col_block = col_ids // blk_size
    col_live = col_ids % blk_size < jnp.take(counts, col_block, axis=0)
    mask_cols = jnp.take(block_mask, col_block, axis=1) == 1
    block_wide = jnp.broadcast_to(mask_cols[:, None, :], (row_blocks, blk_size, col_files)).reshape(
        row_files, col_files
    )
    row_ids = row_index * row_files + lax.iota(jnp.int32, row_files)
    allowed = block_wide & col_live[None, :] & (row_ids[:, None] != col_ids[None, :])
    masked = jnp.where(allowed, scores, -1e30)
    local_top = jnp.max(masked, axis=1)
    row_top = lax.pmax(local_top, "col")
    row_mass = lax.psum(
        jnp.sum(jnp.where(allowed, jnp.exp(masked - row_top[:, None]), 0.0), axis=1), "col"
    )
    weights = jnp.where(allowed, jnp.exp(masked - row_top[:, None]) / row_mass[:, None], 0.0)
    col_mass = lax.psum(jnp.sum(weights, axis=0), "row")
    own_mass = own_piece(col_mass[None, :], col_ratio, n_row, row_index, col_index)[0]
    inv_root = lax.rsqrt((1.0 + own_mass) * 0.5)
    affinity = weights.astype(jnp.bfloat16)
    probe_state = probes
    for sweep in range(ITERS):
        scaled = (probe_state * inv_root[None, :]).astype(jnp.bfloat16)
        probe_rows = lax.all_gather(scaled, "col", axis=1, tiled=True)
        probe_cols = spread(
            lax.dynamic_slice_in_dim(probe_rows, half_pick * col_files, col_files, 1),
            "row",
            col_index // col_ratio,
        )
        row_part = lax.dot_general(
            probe_cols, affinity, (((1,), (1,)), ((), ())), preferred_element_type=jnp.float32
        )
        col_part = jnp.dot(probe_rows, affinity, preferred_element_type=jnp.float32)
        own_rows = lax.psum_scatter(
            row_part.astype(jnp.bfloat16), "col", scatter_dimension=1, tiled=True
        ).astype(jnp.float32)
        col_total = lax.psum(col_part, "row")
        own_cols = own_piece(col_total, col_ratio, n_row, row_index, col_index)
        probe_state = (own_rows + own_cols) * (0.5 * inv_root)[None, :]
    return probe_state


def solution(mesh):
    placed = (
        P(("row", "col"), None),
        P(("row", "col")),
        P("row", None),
        P(),
        P(None, ("row", "col")),
    )
    return jax.shard_map(
        body, mesh=mesh, in_specs=placed, out_specs=P(None, ("row", "col")), check_vma=False
    )
```

profile of v0, /device:TPU:0, one launch (start us, length us, event | category | flops | bytes accessed | tf_op | source)
XLA Modules:
  0.0 495.1 jit_solution(6957773946014642195)
XLA Ops:
  6.5 0.8 copy-done
  7.5 32.7 %all_gather.12 = bf16[256,768]{1,0:T(8,128)(2,1)S(1)} all-gather(bf16[32,768]{1,0:T(8,128)(2,1)S(1)} %fusion.2), channel_id=1, replica_groups=mesh['row'=4,'col'=8] {'col'}, dimensions={0}, use_global_device_ids=true | all-gather | bytes 442368 | tf_op jit(solution)/shard_map/all_gather | solution.py:37
  40.3 0.7 dynamic-slice_select_fusion
  41.2 0.6 copy-done.1
  41.8 0.7 fusion.21
  42.5 0.7 copy-done.3
  43.3 0.6 gather_fusion
  44.3 0.6 copy-done.5
  46.2 0.6 copy-done.4
  47.0 21.5 %all-reduce = bf16[256]{0:T(256)(128)(2,1)S(1)} all-reduce(bf16[256]{0:T(256)(128)(2,1)S(1)} %dynamic-update-slice), channel_id=1, replica_groups=mesh['row'=4,'col'=8] {'col'}, use_global_device_ids=true, to_apply=%add | all-reduce | flops 256 | bytes 1024
  68.5 5.1 %fusion.12 = pred[128]{0:T(512)(128)(4,1)S(1)} fusion(s32[]{:T(128)} %bitcast.3, s32[]{:T(128)} %bitcast.4, s32[]{:T(128)} %bitcast.5, s32[]{:T(128)} %bitcast.6, s32[]{:T(128)} %bitcast.7, s32[]{:T(128)} %bitcast.8, s32[]{:T(128)} %bitcast.9, s32[]{:T(128)} %bitcast.10, s32[]{:T(128)S(6)} %mul.86), kind=kLoop, calls=%fused_computation.62 | loop fusion | flops 7808 | bytes 164 | tf_op jit(solution)/shard_map/lt | solution.py:55
  74.0 1.2 fusion.22
  75.2 21.3 %pmax.7 = f32[256]{0:T(256)S(1)} all-reduce(f32[256]{0:T(256)S(1)} %get-tuple-element.29), channel_id=1, replica_groups=mesh['row'=4,'col'=8] {'col'}, use_global_device_ids=true, to_apply=%region_3.4 | all-reduce | flops 256 | bytes 2048 | tf_op jit(solution)/shard_map/pmax | solution.py:64
  96.7 17.1 %psum.92 = f32[256]{0:T(256)S(1)} all-reduce(f32[256]{0:T(256)S(1)} %select_reduce_fusion), channel_id=1, replica_groups=mesh['row'=4,'col'=8] {'col'}, use_global_device_ids=true, to_apply=%region_5.6 | all-reduce | flops 256 | bytes 2048 | tf_op jit(solution)/shard_map/psum | solution.py:65
  114.0 5.9 %psum.93 = f32[128]{0:T(128)S(1)} all-reduce(f32[128]{0:T(128)S(1)} %get-tuple-element.13), channel_id=1, replica_groups=mesh['row'=4,'col'=8] {'row'}, use_global_device_ids=true, to_apply=%region_7.8 | all-reduce | flops 128 | bytes 1024 | tf_op jit(solution)/shard_map/psum | solution.py:69
  119.9 19.1 %all-reduce.3 = (f32[1,128]{1,0:T(1,128)S(1)}, f32[1,128]{1,0:T(1,128)S(1)}) all-reduce(f32[1,128]{1,0:T(1,128)S(1)} %get-tuple-element.20, f32[1,128]{1,0:T(1,128)S(1)} %get-tuple-element.19), channel_id=1, replica_groups=mesh['row'=4,'col'=8] {'col'}, use_global_device_ids=true, to_apply=%region_8.9 | all-reduce | flops 256 | bytes 2048 | tf_op jit(solution)/shard_map/psum | solution.py:11
  139.2 30.5 %all_gather.14 = bf16[64,256]{0,1:T(8,128)(2,1)S(1)} all-gather(bf16[64,32]{0,1:T(8,128)(2,1)S(1)} %multiply_convert_fusion), channel_id=1, replica_groups=mesh['row'=4,'col'=8] {'col'}, dimensions={1}, use_global_device_ids=true | all-gather | bytes 36864 | tf_op jit(solution)/shard_map/all_gather | solution.py:76
  169.7 10.3 %psum.96 = bf16[64,128]{0,1:T(8,128)(2,1)S(1)} all-reduce(bf16[64,128]{0,1:T(8,128)(2,1)S(1)} %dynamic-slice_select_fusion.2), channel_id=1, replica_groups=mesh['row'=4,'col'=8] {'row'}, use_global_device_ids=true, to_apply=%region_10.11 | all-reduce | flops 8192 | bytes 32768 | tf_op jit(solution)/shard_map/psum | solution.py:11
  180.1 0.8 convolution_convert_fusion.1
  181.0 10.7 %psum.97 = f32[64,128]{0,1:T(8,128)S(1)} all-reduce(f32[64,128]{0,1:T(8,128)S(1)} %fusion.23), channel_id=1, replica_groups=mesh['row'=4,'col'=8] {'row'}, use_global_device_ids=true, to_apply=%region_12.13 | all-reduce | flops 8192 | bytes 65536 | tf_op jit(solution)/shard_map/psum | solution.py:89
  191.8 0.7 broadcast_select_fusion.2
  192.5 46.2 %reduce-scatter.3.cloned.1.call-done = bf16[64,32]{0,1:T(8,128)(2,1)} async-done(((bf16[64,256]{0,1:T(8,128)(2,1)}), bf16[64,32]{0,1:T(8,128)(2,1)}) %reduce-scatter.3.cloned.1.call-update) | async-done | bytes 4112 | tf_op jit(solution)/shard_map/reduce_scatter | solution.py:86
  238.7 72.8 %all-reduce.12.cloned.1.call-done = (f32[64,128]{0,1:T(8,128)}, f32[64,128]{0,1:T(8,128)}) async-done(((f32[64,128]{0,1:T(8,128)}, f32[64,128]{0,1:T(8,128)}), (f32[64,128]{0,1:T(8,128)}, f32[64,128]{0,1:T(8,128)})) %all-reduce.12.cloned.1.call-update) | async-done | bytes 65552 | tf_op jit(solution)/shard_map/psum | solution.py:11
  311.5 0.8 fusion.9
  312.3 30.5 %all_gather.15 = bf16[64,256]{0,1:T(8,128)(2,1)S(1)} all-gather(bf16[64,32]{0,1:T(8,128)(2,1)S(1)} %fusion.9), channel_id=1, replica_groups=mesh['row'=4,'col'=8] {'col'}, dimensions={1}, use_global_device_ids=true | all-gather | bytes 36864 | tf_op jit(solution)/shard_map/all_gather | solution.py:76
  343.0 10.3 %psum.100 = bf16[64,128]{0,1:T(8,128)(2,1)S(1)} all-reduce(bf16[64,128]{0,1:T(8,128)(2,1)S(1)} %dynamic-slice_select_fusion.1), channel_id=1, replica_groups=mesh['row'=4,'col'=8] {'row'}, use_global_device_ids=true, to_apply=%region_15.16 | all-reduce | flops 8192 | bytes 32768 | tf_op jit(solution)/shard_map/psum | solution.py:11
  353.3 0.8 convolution_convert_fusion
  354.2 11.8 %psum.101 = f32[64,128]{0,1:T(8,128)S(1)} all-reduce(f32[64,128]{0,1:T(8,128)S(1)} %fusion.24), channel_id=1, replica_groups=mesh['row'=4,'col'=8] {'row'}, use_global_device_ids=true, to_apply=%region_17.18 | all-reduce | flops 8192 | bytes 65536 | tf_op jit(solution)/shard_map/psum | solution.py:89
  366.0 0.7 broadcast_select_fusion.1
  366.7 48.3 %reduce-scatter.5.cloned.1.call-done = bf16[64,32]{0,1:T(8,128)(2,1)} async-done(((bf16[64,256]{0,1:T(8,128)(2,1)}), bf16[64,32]{0,1:T(8,128)(2,1)}) %reduce-scatter.5.cloned.1.call-update) | async-done | bytes 4112 | tf_op jit(solution)/shard_map/reduce_scatter | solution.py:86
  415.0 72.3 %all-reduce.10.cloned.1.call-done = (f32[64,128]{0,1:T(8,128)}, f32[64,128]{0,1:T(8,128)}) async-done(((f32[64,128]{0,1:T(8,128)}, f32[64,128]{0,1:T(8,128)}), (f32[64,128]{0,1:T(8,128)}, f32[64,128]{0,1:T(8,128)})) %all-reduce.10.cloned.1.call-update) | async-done | bytes 65552 | tf_op jit(solution)/shard_map/psum | solution.py:11
  487.2 1.4 fusion.5
  (45 shorter events, 2.8 us)
Async XLA Ops:
  6.5 0.8 copy-start
  6.5 67.5 %all-reduce.8.cloned.1.call-start = ((), (), s32[]{:S(2)}) async-start(), calls=%async_computation.2 | async-start | bytes 393216 | tf_op jit(solution)/shard_map/psum | solution.py:11
  41.0 197.7 %reduce-scatter.3.cloned.1.call-start = ((), (), s32[]{:S(2)}) async-start(), calls=%async_computation.3 | async-start | bytes 73728 | tf_op jit(solution)/shard_map/reduce_scatter | solution.py:86
  41.2 0.7 copy-start.1
  42.5 0.7 copy-start.3
  44.2 0.7 copy-start.5
  46.1 0.7 copy-start.4
  114.0 25.1 %copy-start.2 = (f32[64,32]{0,1:T(8,128)S(1)}, f32[64,32]{0,1:T(8,128)}, u32[]{:S(2)}) copy-start(f32[64,32]{0,1:T(8,128)} %param.9) | copy-start | bytes 24580
  181.0 130.5 %all-reduce.12.cloned.1.call-start = ((), (), s32[]{:S(2)}) async-start(), calls=%async_computation.6 | async-start | bytes 262144 | tf_op jit(solution)/shard_map/psum | solution.py:11
  192.4 222.5 %reduce-scatter.5.cloned.1.call-start = ((), (), s32[]{:S(2)}) async-start(), calls=%async_computation.4 | async-start | bytes 73728 | tf_op jit(solution)/shard_map/reduce_scatter | solution.py:86
  354.1 133.1 %all-reduce.10.cloned.1.call-start = ((), (), s32[]{:S(2)}) async-start(), calls=%async_computation.5 | async-start | bytes 262144 | tf_op jit(solution)/shard_map/psum | solution.py:11
Sparse Core Ops, SparseCore 0:
  41.1 32.8 all-reduce.7
  181.1 57.5 reduce-scatter.2
  242.6 68.8 all-reduce.11
  354.3 60.6 reduce-scatter.4
  418.3 68.8 all-reduce.9
where the time goes:
time: 496 us; the launch traced here: 495 us
  waiting for transfers between devices  240 us (48%)
  blocking collectives  222 us (45%)
  between operations  14 us (3%)
  other arithmetic  10.2 us (2%)
  local copies, waits for them, and re-layouts  5.8 us (1%)
    psum x3, waiting for transfers between devices, spread(): return lax.psum(jnp.where(mine, shard, jnp.zeros_like(shard)), axis)  145 us
    reduce_scatter x2, waiting for transfers between devices, body(): lax.psum_scatter(row_part.astype(jnp.bfloat16), 'col', scatter_dimension=...  94.5 us
    all_gather x2, blocking collectives, body(): probe_rows = lax.all_gather(scaled, 'col', axis=1, tiled=True)  61 us
    psum x3, blocking collectives, spread(): return lax.psum(jnp.where(mine, shard, jnp.zeros_like(shard)), axis)  39.7 us
    all_gather x1, blocking collectives, body(): lax.all_gather(unit_vec, 'col', axis=0, tiled=True)  32.7 us
    psum x2, blocking collectives, body(): col_total = lax.psum(col_part, 'row')  22.5 us
    unnamed x1, blocking collectives  21.5 us
    pmax x1, blocking collectives, body(): row_top = lax.pmax(local_top, 'col')  21.3 us
  transfers between devices with their start and end apart: 5, of which 5 were waited for; matrix products, arithmetic and copies ran while one was open for 2% of the time, Pallas kernels for 0%

commit v1 on v0

--- a/solution.py
+++ b/solution.py
@@ -73,7 +73,23 @@
     probe_state = probes
     for sweep in range(ITERS):
         scaled = (probe_state * inv_root[None, :]).astype(jnp.bfloat16)
-        probe_rows = lax.all_gather(scaled, "col", axis=1, tiled=True)
+
+        def _guide_limits(array_here):
+            kept_arr, vec_out = (lax.axis_size("col"), lax.axis_index("col"))
+            moved, main = (array_here, 1)
+            while main < kept_arr:
+                passed = lax.ppermute(
+                    moved,
+                    axis_name="col",
+                    perm=[(dev_i, dev_i ^ main) for dev_i in range(kept_arr)],
+                )
+                next_value = jnp.concatenate([moved, passed], 1)
+                b_now = jnp.concatenate([passed, moved], 1)
+                moved = jnp.where(vec_out & main == 0, next_value, b_now)
+                main = 2 * main
+            return moved
+
+        probe_rows = _guide_limits(scaled)
         probe_cols = spread(
             lax.dynamic_slice_in_dim(probe_rows, half_pick * col_files, col_files, 1),
             "row",

time: 496 us -> 460 us (0.927)
  blocking collectives: 222 us -> 160 us
  waiting for transfers between devices: 240 us -> 261 us
    all_gather x2 -> x0, blocking collectives: 61 us -> none  [body(): probe_rows = lax.all_gather(scaled, 'col', axis=1, tiled=True)]
    ppermute x0 -> x6, waiting for transfers between devices: none -> 20.9 us  [_guide_limits(): lax.ppermute(moved, axis_name='col', perm=[(dev_i, dev_i ^ main) for dev_...]
  transfers between devices with their start and end apart: 5 -> 11, of which waited for: 5 -> 11; matrix products, arithmetic and copies ran while one was open for 2% -> 2% of each run, Pallas kernels for 0% -> 0%
where the time goes in v1:
time: 460 us; the launch traced here: 459 us
  waiting for transfers between devices  261 us (57%)
  blocking collectives  160 us (35%)
  between operations  14.1 us (3%)
  other arithmetic  10.3 us (2%)
  local copies, waits for them, and re-layouts  5.8 us (1%)
    psum x3, waiting for transfers between devices, spread(): return lax.psum(jnp.where(mine, shard, jnp.zeros_like(shard)), axis)  145 us
    reduce_scatter x2, waiting for transfers between devices, body(): lax.psum_scatter(row_part.astype(jnp.bfloat16), 'col', scatter_dimension=...  95 us
    psum x3, blocking collectives, spread(): return lax.psum(jnp.where(mine, shard, jnp.zeros_like(shard)), axis)  39.7 us
    all_gather x1, blocking collectives, body(): lax.all_gather(unit_vec, 'col', axis=0, tiled=True)  32.7 us
    psum x2, blocking collectives, body(): col_total = lax.psum(col_part, 'row')  22.1 us
    unnamed x1, blocking collectives  21.5 us
    pmax x1, blocking collectives, body(): row_top = lax.pmax(local_top, 'col')  21.3 us
    ppermute x6, waiting for transfers between devices, _guide_limits(): lax.ppermute(moved, axis_name='col', perm=[(dev_i, dev_i ^ main) for dev_...  20.9 us
  transfers between devices with their start and end apart: 11, of which 11 were waited for; matrix products, arithmetic and copies ran while one was open for 2% of the time, Pallas kernels for 0%

profile of v1, /device:TPU:0, one launch (start us, length us, event | category | flops | bytes accessed | tf_op | source)
XLA Modules:
  0.0 459.0 jit_solution(12735307957406408422)
XLA Ops:
  6.5 0.8 copy-done
  7.5 32.7 %all_gather.6 = bf16[256,768]{1,0:T(8,128)(2,1)S(1)} all-gather(bf16[32,768]{1,0:T(8,128)(2,1)S(1)} %fusion.2), channel_id=1, replica_groups=mesh['row'=4,'col'=8] {'col'}, dimensions={0}, use_global_device_ids=true | all-gather | bytes 442368 | tf_op jit(solution)/shard_map/all_gather | solution.py:37
  40.3 0.7 dynamic-slice_select_fusion
  41.8 0.7 fusion.21
  47.0 21.5 %all-reduce = bf16[256]{0:T(256)(128)(2,1)S(1)} all-reduce(bf16[256]{0:T(256)(128)(2,1)S(1)} %dynamic-update-slice), channel_id=1, replica_groups=mesh['row'=4,'col'=8] {'col'}, use_global_device_ids=true, to_apply=%add | all-reduce | flops 256 | bytes 1024
  68.5 5.1 %fusion.12 = pred[128]{0:T(512)(128)(4,1)S(1)} fusion(s32[]{:T(128)} %bitcast.3, s32[]{:T(128)} %bitcast.4, s32[]{:T(128)} %bitcast.5, s32[]{:T(128)} %bitcast.6, s32[]{:T(128)} %bitcast.7, s32[]{:T(128)} %bitcast.8, s32[]{:T(128)} %bitcast.9, s32[]{:T(128)} %bitcast.10, s32[]{:T(128)S(6)} %mul.86), kind=kLoop, calls=%fused_computation.68 | loop fusion | flops 7808 | bytes 164 | tf_op jit(solution)/shard_map/lt | solution.py:55
  74.0 1.2 fusion.22
  75.2 21.3 %pmax.7 = f32[256]{0:T(256)S(1)} all-reduce(f32[256]{0:T(256)S(1)} %get-tuple-element.29), channel_id=1, replica_groups=mesh['row'=4,'col'=8] {'col'}, use_global_device_ids=true, to_apply=%region_3.4 | all-reduce | flops 256 | bytes 2048 | tf_op jit(solution)/shard_map/pmax | solution.py:64
  96.7 17.1 %psum.92 = f32[256]{0:T(256)S(1)} all-reduce(f32[256]{0:T(256)S(1)} %select_reduce_fusion), channel_id=1, replica_groups=mesh['row'=4,'col'=8] {'col'}, use_global_device_ids=true, to_apply=%region_5.6 | all-reduce | flops 256 | bytes 2048 | tf_op jit(solution)/shard_map/psum | solution.py:65
  114.0 5.9 %psum.93 = f32[128]{0:T(128)S(1)} all-reduce(f32[128]{0:T(128)S(1)} %get-tuple-element.13), channel_id=1, replica_groups=mesh['row'=4,'col'=8] {'row'}, use_global_device_ids=true, to_apply=%region_7.8 | all-reduce | flops 128 | bytes 1024 | tf_op jit(solution)/shard_map/psum | solution.py:69
  119.9 19.1 %all-reduce.3 = (f32[1,128]{1,0:T(1,128)S(1)}, f32[1,128]{1,0:T(1,128)S(1)}) all-reduce(f32[1,128]{1,0:T(1,128)S(1)} %get-tuple-element.20, f32[1,128]{1,0:T(1,128)S(1)} %get-tuple-element.19), channel_id=1, replica_groups=mesh['row'=4,'col'=8] {'col'}, use_global_device_ids=true, to_apply=%region_8.9 | all-reduce | flops 256 | bytes 2048 | tf_op jit(solution)/shard_map/psum | solution.py:11
  139.2 3.6 collective-permute-done
  142.9 3.7 collective-permute-done.1
  146.8 4.8 %collective-permute-done.2 = bf16[64,128]{0,1:T(8,128)(2,1)S(1)} collective-permute-done((bf16[64,128]{0,1:T(8,128)(2,1)S(1)}, bf16[64,128]{0,1:T(8,128)(2,1)S(1)}, u32[]{:S(2)}, u32[]{:S(2)}) %collective-permute-start.2) | collective-permute-done | bytes 16416 | tf_op jit(solution)/shard_map/ppermute | solution.py:81
  151.6 10.3 %psum.96 = bf16[64,128]{0,1:T(8,128)(2,1)S(1)} all-reduce(bf16[64,128]{0,1:T(8,128)(2,1)S(1)} %dynamic-slice_select_fusion.2), channel_id=1, replica_groups=mesh['row'=4,'col'=8] {'row'}, use_global_device_ids=true, to_apply=%region_10.11 | all-reduce | flops 8192 | bytes 32768 | tf_op jit(solution)/shard_map/psum | solution.py:11
  162.0 0.8 convolution_convert_fusion.1
  163.0 10.7 %psum.97 = f32[64,128]{0,1:T(8,128)S(1)} all-reduce(f32[64,128]{0,1:T(8,128)S(1)} %fusion.23), channel_id=1, replica_groups=mesh['row'=4,'col'=8] {'row'}, use_global_device_ids=true, to_apply=%region_12.13 | all-reduce | flops 8192 | bytes 65536 | tf_op jit(solution)/shard_map/psum | solution.py:105
  174.4 46.0 %reduce-scatter.3.cloned.1.call-done = bf16[64,32]{0,1:T(8,128)(2,1)} async-done(((bf16[64,256]{0,1:T(8,128)(2,1)}), bf16[64,32]{0,1:T(8,128)(2,1)}) %reduce-scatter.3.cloned.1.call-update) | async-done | bytes 4112 | tf_op jit(solution)/shard_map/reduce_scatter | solution.py:102
  220.4 72.8 %all-reduce.12.cloned.1.call-done = (f32[64,128]{0,1:T(8,128)}, f32[64,128]{0,1:T(8,128)}) async-done(((f32[64,128]{0,1:T(8,128)}, f32[64,128]{0,1:T(8,128)}), (f32[64,128]{0,1:T(8,128)}, f32[64,128]{0,1:T(8,128)})) %all-reduce.12.cloned.1.call-update) | async-done | bytes 65552 | tf_op jit(solution)/shard_map/psum | solution.py:11
  293.2 0.8 fusion.9
  294.0 0.8 collective-permute-start.3
  294.8 2.9 collective-permute-done.3
  297.7 1.1 collective-permute-start.4
  298.7 2.7 collective-permute-done.4
  301.5 1.8 collective-permute-start.5
  303.3 3.1 collective-permute-done.5
  306.6 10.3 %psum.100 = bf16[64,128]{0,1:T(8,128)(2,1)S(1)} all-reduce(bf16[64,128]{0,1:T(8,128)(2,1)S(1)} %dynamic-slice_select_fusion.1), channel_id=1, replica_groups=mesh['row'=4,'col'=8] {'row'}, use_global_device_ids=true, to_apply=%region_15.16 | all-reduce | flops 8192 | bytes 32768 | tf_op jit(solution)/shard_map/psum | solution.py:11
  316.8 0.8 convolution_convert_fusion
  317.8 11.4 %psum.101 = f32[64,128]{0,1:T(8,128)S(1)} all-reduce(f32[64,128]{0,1:T(8,128)S(1)} %fusion.24), channel_id=1, replica_groups=mesh['row'=4,'col'=8] {'row'}, use_global_device_ids=true, to_apply=%region_17.18 | all-reduce | flops 8192 | bytes 65536 | tf_op jit(solution)/shard_map/psum | solution.py:105
  329.8 49.0 %reduce-scatter.5.cloned.1.call-done = bf16[64,32]{0,1:T(8,128)(2,1)} async-done(((bf16[64,256]{0,1:T(8,128)(2,1)}), bf16[64,32]{0,1:T(8,128)(2,1)}) %reduce-scatter.5.cloned.1.call-update) | async-done | bytes 4112 | tf_op jit(solution)/shard_map/reduce_scatter | solution.py:102
  378.8 72.2 %all-reduce.10.cloned.1.call-done = (f32[64,128]{0,1:T(8,128)}, f32[64,128]{0,1:T(8,128)}) async-done(((f32[64,128]{0,1:T(8,128)}, f32[64,128]{0,1:T(8,128)}), (f32[64,128]{0,1:T(8,128)}, f32[64,128]{0,1:T(8,128)})) %all-reduce.10.cloned.1.call-update) | async-done | bytes 65552 | tf_op jit(solution)/shard_map/psum | solution.py:11
  451.0 1.4 fusion.5
  (61 shorter events, 7.6 us)
Async XLA Ops:
  6.5 0.8 copy-start
  6.5 67.5 %all-reduce.8.cloned.1.call-start = ((), (), s32[]{:S(2)}) async-start(), calls=%async_computation.2 | async-start | bytes 393216 | tf_op jit(solution)/shard_map/psum | solution.py:11
  41.0 179.4 %reduce-scatter.3.cloned.1.call-start = ((), (), s32[]{:S(2)}) async-start(), calls=%async_computation.3 | async-start | bytes 73728 | tf_op jit(solution)/shard_map/reduce_scatter | solution.py:102
  41.2 0.7 copy-start.1
  42.5 0.7 copy-start.3
  44.2 0.7 copy-start.5
  46.1 0.7 copy-start.4
  114.0 25.1 %copy-start.2 = (f32[64,32]{0,1:T(8,128)S(1)}, f32[64,32]{0,1:T(8,128)}, u32[]{:S(2)}) copy-start(f32[64,32]{0,1:T(8,128)} %param.9) | copy-start | bytes 24580
  139.2 3.7 collective-permute-start
  142.9 3.8 collective-permute-start.1
  146.7 4.9 %collective-permute-start.2 = (bf16[64,128]{0,1:T(8,128)(2,1)S(1)}, bf16[64,128]{0,1:T(8,128)(2,1)S(1)}, u32[]{:S(2)}, u32[]{:S(2)}) collective-permute-start(bf16[64,128]{0,1:T(8,128)(2,1)S(1)} %maximum_select_fusion.2), channel_id=1, source_target_pairs={{0,4},{1,5},{2,6},{3,7},{4,0},{5,1},{6,2},{7,3},{8,12},{9,13},{10,... | collective-permute-start | bytes 49160 | tf_op jit(solution)/shard_map/ppermute | solution.py:81
  162.9 130.3 %all-reduce.12.cloned.1.call-start = ((), (), s32[]{:S(2)}) async-start(), calls=%async_computation.6 | async-start | bytes 262144 | tf_op jit(solution)/shard_map/psum | solution.py:11
  174.3 204.5 %reduce-scatter.5.cloned.1.call-start = ((), (), s32[]{:S(2)}) async-start(), calls=%async_computation.4 | async-start | bytes 73728 | tf_op jit(solution)/shard_map/reduce_scatter | solution.py:102
  294.0 3.7 collective-permute-start.3
  297.7 3.8 collective-permute-start.4
  301.5 4.9 %collective-permute-start.5 = (bf16[64,128]{0,1:T(8,128)(2,1)S(1)}, bf16[64,128]{0,1:T(8,128)(2,1)S(1)}, u32[]{:S(2)}, u32[]{:S(2)}) collective-permute-start(bf16[64,128]{0,1:T(8,128)(2,1)S(1)} %maximum_select_fusion.3), channel_id=1, source_target_pairs={{0,4},{1,5},{2,6},{3,7},{4,0},{5,1},{6,2},{7,3},{8,12},{9,13},{10,... | collective-permute-start | bytes 49160 | tf_op jit(solution)/shard_map/ppermute | solution.py:81
  317.7 133.3 %all-reduce.10.cloned.1.call-start = ((), (), s32[]{:S(2)}) async-start(), calls=%async_computation.5 | async-start | bytes 262144 | tf_op jit(solution)/shard_map/psum | solution.py:11
Sparse Core Ops, SparseCore 0:
  41.1 32.8 all-reduce.7
  163.0 57.3 reduce-scatter.2
  224.3 68.8 all-reduce.11
  317.8 60.9 reduce-scatter.4
  382.1 68.8 all-reduce.9
